TPU v7x, 512 devices: a whole 4x8x8 slice. The times are simulated.
512 devices in a mesh: tm: 64 (over z, x, y_hi), chan: 8 (over y_lo, core).
Axes of the slice: x: 4, y: 8 (y_hi: 2, y_lo: 4; y = y_hi * 4 + y_lo), z: 8, core: 2. Of those that a mesh axis runs over, the one named last changes fastest.
Arguments:
- field: float32 [2, 2, 64, 65536], P(None, None, 'chan', 'tm'), may hold values from -15.5 to 15.5
- noise: float32 [1, 2, 2, 64, 65536], P(None, None, None, 'chan', 'tm'), may hold values from -1.25 to 1.25
- assign: int32 [64], P('chan'), may hold values from 0 to 63, each once
Outputs:
- received: float32 [2, 2, 64, 65536], P(None, None, 'chan', 'tm')
- recovered: float32 [2, 2, 64, 65536], P(None, None, 'chan', 'tm')
All inputs are finite; a program needn't handle non-finite values.
Results may differ from a plain program's by a relative error of at most 0.0003.
Values sent between devices are 32-bit elements; how exact they have to be, the bound alone decides.
No kernel may reach another device: no remote copies, remote signals or barrier semaphores. Data moves between devices by JAX's collectives and lax.ppermute only.
A program may use at most 64 MiB of HBM per device.

v0:
```python
import jax
import jax.numpy as jnp
from jax import lax
from jax.sharding import Mesh, PartitionSpec as P

OPTICAL_CHANNELS = 64
FILTER_HALF_TAPS = 128
STEPS = 2
FIBER_SECTIONS = 1
ATT = 0.955
GAMMA = 0.004
WALK = 0.5
SPREAD = 0.4
CHIRP = 0.25
EPS = 1e-06


def tap_tables(channel_ids, sign, reach, channels):
    rows = jnp.arange(3 * reach, dtype=jnp.int32)[:, None]
    cols = jnp.arange(reach, dtype=jnp.int32)[None, :]
    lag = cols - rows + reach
    interior_part = (jnp.abs(lag) <= reach).astype(jnp.float32)
    centre = (
        WALK * reach * (2.0 * channel_ids.astype(jnp.float32) - (channels - 1)) / (channels - 1)
    )
    centre = centre[:, None, None]
    width = SPREAD * reach
    offset = sign * lag.astype(jnp.float32)[None] - centre
    symbol_profile = jnp.exp(-jnp.square(offset / width))
    turn = jnp.square(offset) / (2.0 * CHIRP * reach)
    taps = jnp.arange(-reach, reach + 1, dtype=jnp.int32).astype(jnp.float32)
    scale = jnp.sqrt(
        jnp.sum(jnp.exp(-2.0 * jnp.square((taps[None, :] - centre[:, :, 0]) / width)), axis=1)
    )
    scale = scale[:, None, None]
    mat_re = interior_part * symbol_profile * jnp.cos(turn) / scale
    mat_im = sign * interior_part * symbol_profile * jnp.sin(turn) / scale
    return (mat_re, mat_im)


def merged_table(mat_re, mat_im):
    top = jnp.concatenate([mat_re, mat_im], axis=2)
    bottom = jnp.concatenate([-mat_im, mat_re], axis=2)
    return jnp.concatenate([top, bottom], axis=1)


def disperse(ext, table, reach):
    pols, parts, chans, segment_length = ext.shape
    blocks = segment_length // reach - 2
    rows = ext.reshape(pols, parts, chans, blocks + 2, reach)
    window = jnp.concatenate(
        [rows[:, :, :, 0:blocks], rows[:, :, :, 1 : blocks + 1], rows[:, :, :, 2 : blocks + 2]],
        axis=4,
    )
    stacked = jnp.moveaxis(window, 1, 3).reshape(pols, chans, blocks, parts * 3 * reach)
    out = jnp.einsum("pcjq,cqn->pcjn", stacked, table, precision=lax.Precision.HIGHEST)
    out = jnp.moveaxis(out.reshape(pols, chans, blocks, parts, reach), 3, 1)
    return out.reshape(pols, parts, chans, blocks * reach)


def rotate(ext, sign, own, total):
    angle = sign * GAMMA * (2.0 * total[None, :] - own)
    cosine = jnp.cos(angle)
    sine = jnp.sin(angle)
    real = ext[:, 0]
    imag = ext[:, 1]
    return jnp.stack([real * cosine - imag * sine, real * sine + imag * cosine], axis=1)


TM = ("z", "x", "yh")
CHAN = ("ylo", "core")


def psum_tm(value):
    for axis in ("yh", "x", "z"):
        value = lax.psum(value, axis)
    return value


def psum_chan(value):
    for axis in ("core", "ylo"):
        value = lax.psum(value, axis)
    return value


def on_device(field, noise, assign):
    forward, backward = lax.optimization_barrier(
        (
            merged_table(*tap_tables(assign, 1.0, FILTER_HALF_TAPS, OPTICAL_CHANNELS)),
            merged_table(*tap_tables(assign, -1.0, FILTER_HALF_TAPS, OPTICAL_CHANNELS)),
        )
    )
    total_len = lax.axis_size(TM) * field.shape[3]
    reach = FILTER_HALF_TAPS
    field_width = 2 * STEPS * reach
    noise_width = STEPS * reach

    def nonlinear(ext, sign):
        own = jnp.sum(jnp.square(ext), axis=(0, 1))
        total = psum_chan(jnp.sum(own, axis=0))
        return rotate(ext, sign, own, total)

    last_noise = noise[FIBER_SECTIONS - 1]
    count, length = (lax.axis_size(TM), field.shape[3])
    up = [(i, (i + 1) % count) for i in range(count)]
    down = [(j, i) for i, j in up]
    trailing = jnp.concatenate(
        [field[..., length - field_width :], last_noise[..., length - noise_width :]], axis=3
    )
    leading = jnp.concatenate([field[..., :field_width], last_noise[..., :noise_width]], axis=3)
    before = lax.ppermute(trailing, TM, up)
    after = lax.ppermute(leading, TM, down)
    current = jnp.concatenate([before[..., :field_width], field, after[..., :field_width]], axis=3)
    noise_ext = jnp.concatenate(
        [before[..., field_width:], last_noise, after[..., field_width:]], axis=3
    )
    for step in range(STEPS):
        current = disperse(current, forward, reach) * ATT
        current = nonlinear(current, 1.0)
    centre = slice(noise_width, noise_width + length)
    signal, added = (current[..., centre], last_noise)
    sums = psum_tm(
        jnp.stack(
            [
                jnp.sum(jnp.square(signal), axis=(0, 1, 3)),
                jnp.sum(signal * added, axis=(0, 1, 3)),
                jnp.sum(jnp.square(added), axis=(0, 1, 3)),
            ]
        )
    )
    gain = lax.rsqrt(sums[0] / total_len + EPS)
    arrival = (gain * gain * sums[0] + 2.0 * gain * sums[1] + sums[2]) / total_len
    current = current * gain[None, None, :, None] + noise_ext
    received = current[..., centre]
    rescale = jnp.sqrt(ATT ** (2 * STEPS) / (arrival + EPS))
    current = current * rescale[None, None, :, None]
    for step in range(STEPS):
        current = nonlinear(current, -1.0) / ATT
        current = disperse(current, backward, reach)
    return (received, current)


def solution(mesh):
    tm, chan = (mesh.shape["tm"], mesh.shape["chan"])
    fine = Mesh(mesh.devices.reshape(tm // 16, 8, 2, chan // 2, 2), TM + CHAN)
    placed = (P(None, None, CHAN, TM), P(None, None, None, CHAN, TM), P(CHAN))
    return jax.shard_map(
        on_device,
        mesh=fine,
        in_specs=placed,
        out_specs=(P(None, None, CHAN, TM), P(None, None, CHAN, TM)),
        check_vma=False,
    )
```

profile of v0, /device:TPU:8, one launch (start us, length us, event | category | flops | bytes accessed | tf_op | source)
XLA Modules:
  0.0 157.8 jit_solution(16434985247068703220)
XLA Ops:
  0.6 0.8 fusion.85
  1.4 0.9 fusion.84
  2.3 6.8 %collective-permute-start = (f32[2,2,8,768]{3,2,1,0:T(8,128)S(1)}, f32[2,2,8,768]{3,2,1,0:T(8,128)S(1)}, u32[]{:S(2)}, u32[]{:S(2)}) collective-permute-start(f32[2,2,8,768]{3,2,1,0:T(8,128)S(1)} %pad_maximum_fusion.2), channel_id=1, source_target_pairs={{0,8},{8,16},{16,24},{24,32},{32,40},{40,48},{48,56},{56,64},{64,7... | collective-permute-start | bytes 294920 | tf_op jit(solution)/shard_map/ppermute | solution.py:111
  9.2 12.6 %collective-permute-start.1 = (f32[2,2,8,768]{3,2,1,0:T(8,128)S(1)}, f32[2,2,8,768]{3,2,1,0:T(8,128)S(1)}, u32[]{:S(2)}, u32[]{:S(2)}) collective-permute-start(f32[2,2,8,768]{3,2,1,0:T(8,128)S(1)} %pad_maximum_fusion.3), channel_id=1, source_target_pairs={{8,0},{16,8},{24,16},{32,24},{40,32},{48,40},{56,48},{64,56},{72,6... | collective-permute-start | bytes 294920 | tf_op jit(solution)/shard_map/ppermute | solution.py:112
  22.0 0.2 exponential_reduce_fusion
  22.2 12.3 %fusion.27 = (f32[8,384,128]{2,1,0:T(8,128)S(1)}, f32[8,384,128]{2,1,0:T(8,128)S(1)}, f32[8,384,128]{2,1,0:T(8,128)S(1)}, f32[8,384,128]{2,1,0:T(8,128)S(1)}, f3...) fusion(f32[384,128]{1,0:T(8,128)S(1)} %fusion.62, f32[384,128]{1,0:T(8,128)S(1)} %broadcast_multiply_fusion.1, ...), kind=kLoop, calls=%fused_computation.33 | loop fusion | flops 9830400 | bytes 10223680 | tf_op jit(solution)/shard_map/div | solution.py:37
  34.5 5.1 %maximum_maximum_fusion = (f32[8,768,256]{2,1,0:T(8,128)}, f32[8,768,256]{2,1,0:T(8,128)}) fusion(f32[8,384,128]{2,1,0:T(8,128)S(1)} %get-tuple-element.39, f32[8,384,128]{2,1,0:T(8,128)S(1)} %get-tuple-element.40, f32[8,384,128]{2,1,0:T(8,128)S(1)} %get-tuple-element.41, f32[8,384,128]{2,1,0:T(8,128)S(1)} %get-tuple-element.38, ...), kind=kLoop, calls=%fused_computation | loop fusion | flops 9437184 | bytes 22020096 | tf_op jit(solution)/shard_map/concatenate | solution.py:44
  39.8 0.1 copy.89
  39.9 0.1 copy.90
  40.1 0.1 copy.91
  40.2 0.3 maximum_bitcast_fusion
  40.5 0.6 reshape.320
  41.0 6.1 %multiply_reduce_fusion.3 = (f32[14,256]{1,0:T(8,128)S(1)}, f32[8,14,256]{2,1,0:T(8,128)S(1)}, f32[2,8,14,256]{3,2,0,1:T(8,128)S(1)}) fusion(f32[2,8,14,768]{3,1,2,0:T(8,128)S(1)} %reshape.320, f32[8,768,256]{2,1,0:T(8,128)} %get-tuple-element.4), kind=kOutput, calls=%fused_computation.56 | convolution fusion | flops 528679424 | bytes 7337984 | tf_op jit(solution)/shard_map/pcjq,cqn->pcjn/dot_general | solution.py:56
  47.1 0.1 bitcast_reduce_fusion
  47.2 2.5 %psum.77 = f32[1792]{0:T(1024)S(1)} all-reduce(f32[1792]{0:T(1024)S(1)} %bitcast.178), channel_id=1, replica_groups=mesh['z'=4,'x'=8,'yh'=2,'ylo'=4,'core'=2] {'core'}, use_global_device_ids=true, to_apply=%region_3.0 | all-reduce | flops 1792 | bytes 14336 | tf_op jit(solution)/shard_map/psum | solution.py:82
  49.8 9.9 %psum.78 = f32[1792]{0:T(1024)S(1)} all-reduce(f32[1792]{0:T(1024)S(1)} %psum.77), channel_id=1, replica_groups=mesh['z'=4,'x'=8,'yh'=2,'ylo'=4,'core'=2] {'ylo'}, use_global_device_ids=true, to_apply=%region_4.0 | all-reduce | flops 1792 | bytes 14336 | tf_op jit(solution)/shard_map/psum | solution.py:82
  59.7 0.1 copy_bitcast_fusion
  59.8 0.2 fusion.66
  60.1 0.2 fusion.55
  60.3 0.4 fusion.53
  60.7 0.5 reshape.321
  61.2 6.1 %multiply_reduce_fusion.1 = (f32[12,256]{1,0:T(8,128)S(1)}, f32[8,12,256]{2,1,0:T(8,128)S(1)}, f32[2,8,12,256]{3,2,0,1:T(8,128)S(1)}) fusion(f32[2,8,12,768]{3,1,2,0:T(8,128)S(1)} %reshape.321, f32[8,768,256]{2,1,0:T(8,128)} %get-tuple-element.4), kind=kOutput, calls=%fused_computation.54 | convolution fusion | flops 453153792 | bytes 7188480 | tf_op jit(solution)/shard_map/pcjq,cqn->pcjn/dot_general | solution.py:56
  67.3 0.1 bitcast_reduce_fusion.1
  67.4 2.5 %psum.79 = f32[1536]{0:T(1024)S(1)} all-reduce(f32[1536]{0:T(1024)S(1)} %bitcast.179), channel_id=1, replica_groups=mesh['z'=4,'x'=8,'yh'=2,'ylo'=4,'core'=2] {'core'}, use_global_device_ids=true, to_apply=%region_9.0 | all-reduce | flops 1536 | bytes 12288 | tf_op jit(solution)/shard_map/psum | solution.py:82
  69.9 9.4 %psum.80 = f32[1536]{0:T(1024)S(1)} all-reduce(f32[1536]{0:T(1024)S(1)} %psum.79), channel_id=1, replica_groups=mesh['z'=4,'x'=8,'yh'=2,'ylo'=4,'core'=2] {'ylo'}, use_global_device_ids=true, to_apply=%region_10.0 | all-reduce | flops 1536 | bytes 12288 | tf_op jit(solution)/shard_map/psum | solution.py:82
  79.3 0.1 copy_bitcast_fusion.2
  79.5 0.2 fusion.71
  79.7 0.2 multiply_reduce_fusion.10
  79.9 8.8 %psum.81 = f32[3,8]{1,0:T(4,128)S(1)} all-reduce(f32[3,8]{1,0:T(4,128)S(1)} %pad_maximum_fusion.4), channel_id=1, replica_groups=mesh['z'=4,'x'=8,'yh'=2,'ylo'=4,'core'=2] {'yh'}, use_global_device_ids=true, to_apply=%region_16.0 | all-reduce | flops 24 | bytes 192 | tf_op jit(solution)/shard_map/psum | solution.py:76
  88.7 16.0 %psum.82 = f32[3,8]{1,0:T(4,128)S(1)} all-reduce(f32[3,8]{1,0:T(4,128)S(1)} %psum.81), channel_id=1, replica_groups=mesh['z'=4,'x'=8,'yh'=2,'ylo'=4,'core'=2] {'x'}, use_global_device_ids=true, to_apply=%region_17.0 | all-reduce | flops 24 | bytes 192 | tf_op jit(solution)/shard_map/psum | solution.py:76
  104.7 14.3 %psum.83 = f32[3,8]{1,0:T(4,128)S(1)} all-reduce(f32[3,8]{1,0:T(4,128)S(1)} %psum.82), channel_id=1, replica_groups=mesh['z'=4,'x'=8,'yh'=2,'ylo'=4,'core'=2] {'z'}, use_global_device_ids=true, to_apply=%region_18.0 | all-reduce | flops 24 | bytes 192 | tf_op jit(solution)/shard_map/psum | solution.py:76
  119.1 0.1 multiply_reduce_fusion.5
  119.2 2.5 %psum.84 = f32[1536]{0:T(1024)S(1)} all-reduce(f32[1536]{0:T(1024)S(1)} %get-tuple-element.10), channel_id=1, replica_groups=mesh['z'=4,'x'=8,'yh'=2,'ylo'=4,'core'=2] {'core'}, use_global_device_ids=true, to_apply=%region_20.0 | all-reduce | flops 1536 | bytes 12288 | tf_op jit(solution)/shard_map/psum | solution.py:82
  121.7 8.5 %psum.85 = f32[1536]{0:T(1024)S(1)} all-reduce(f32[1536]{0:T(1024)S(1)} %psum.84), channel_id=1, replica_groups=mesh['z'=4,'x'=8,'yh'=2,'ylo'=4,'core'=2] {'ylo'}, use_global_device_ids=true, to_apply=%region_21.0 | all-reduce | flops 1536 | bytes 12288 | tf_op jit(solution)/shard_map/psum | solution.py:82
  130.3 0.2 fusion.69
  130.5 0.2 maximum_multiply_fusion
  130.7 0.1 fusion.82
  130.9 0.2 maximum_bitcast_fusion.1
  131.1 0.4 reshape.322
  131.5 6.0 %fusion.43 = f32[2,8,10,256]{3,2,0,1:T(8,128)S(1)} fusion(f32[8,768,256]{2,1,0:T(8,128)} %get-tuple-element.5, f32[2,8,10,768]{3,1,2,0:T(8,128)S(1)} %reshape.322), kind=kOutput, calls=%fused_computation.41 | convolution fusion | flops 377487360 | bytes 6946816 | tf_op jit(solution)/shard_map/pcjq,cqn->pcjn/dot_general | solution.py:56
  137.5 0.1 multiply_reduce_fusion.7
  137.6 2.5 %psum.86 = f32[1280]{0:T(1024)S(1)} all-reduce(f32[1280]{0:T(1024)S(1)} %bitcast.180), channel_id=1, replica_groups=mesh['z'=4,'x'=8,'yh'=2,'ylo'=4,'core'=2] {'core'}, use_global_device_ids=true, to_apply=%region_24.25 | all-reduce | flops 1280 | bytes 10240 | tf_op jit(solution)/shard_map/psum | solution.py:82
  140.1 10.5 %psum.87 = f32[1280]{0:T(1024)S(1)} all-reduce(f32[1280]{0:T(1024)S(1)} %psum.86), channel_id=1, replica_groups=mesh['z'=4,'x'=8,'yh'=2,'ylo'=4,'core'=2] {'ylo'}, use_global_device_ids=true, to_apply=%region_25.26 | all-reduce | flops 1280 | bytes 10240 | tf_op jit(solution)/shard_map/psum | solution.py:82
  150.6 0.2 fusion.74
  150.9 0.1 copy.85
  151.0 5.4 %fusion.46 = f32[2,2,8,8,128]{4,3,1,0,2:T(8,128)S(1)} fusion(f32[2,8,8,768]{3,2,0,1:T(8,128)S(1)} %bitcast.167, f32[8,768,256]{2,1,0:T(8,128)} %get-tuple-element.5), kind=kOutput, calls=%fused_computation.42 | convolution fusion | flops 301989888 | bytes 6815744 | tf_op jit(solution)/shard_map/pcjq,cqn->pcjn/dot_general | solution.py:56
  156.4 0.7 copy.115
  157.2 0.7 slice.152
  (41 shorter events, 0.6 us)
Async XLA Ops:
  0.6 21.4 %copy-start.2 = (s32[8]{0:T(128)S(1)}, s32[8]{0:T(128)}, u32[]{:S(2)}) copy-start(s32[8]{0:T(128)} %param.5) | copy-start | bytes 100
  2.3 37.3 %collective-permute-start = (f32[2,2,8,768]{3,2,1,0:T(8,128)S(1)}, f32[2,2,8,768]{3,2,1,0:T(8,128)S(1)}, u32[]{:S(2)}, u32[]{:S(2)}) collective-permute-start(f32[2,2,8,768]{3,2,1,0:T(8,128)S(1)} %pad_maximum_fusion.2), channel_id=1, source_target_pairs={{0,8},{8,16},{16,24},{24,32},{32,40},{40,48},{48,56},{56,64},{64,7... | collective-permute-start | bytes 294920 | tf_op jit(solution)/shard_map/ppermute | solution.py:111
  9.2 30.5 %collective-permute-start.1 = (f32[2,2,8,768]{3,2,1,0:T(8,128)S(1)}, f32[2,2,8,768]{3,2,1,0:T(8,128)S(1)}, u32[]{:S(2)}, u32[]{:S(2)}) collective-permute-start(f32[2,2,8,768]{3,2,1,0:T(8,128)S(1)} %pad_maximum_fusion.3), channel_id=1, source_target_pairs={{8,0},{16,8},{24,16},{32,24},{40,32},{48,40},{56,48},{64,56},{72,6... | collective-permute-start | bytes 294920 | tf_op jit(solution)/shard_map/ppermute | solution.py:112
  34.5 5.2 %copy-start.1 = (f32[2,2,8,1024]{3,2,1,0:T(8,128)S(1)}, f32[2,2,8,1024]{3,2,1,0:T(8,128)}, u32[]{:S(2)}) copy-start(f32[2,2,8,1024]{3,2,1,0:T(8,128)} %param.3) | copy-start | bytes 393220
  61.2 18.5 %copy-start = (f32[1,2,2,8,1024]{4,3,2,1,0:T(8,128)S(1)}, f32[1,2,2,8,1024]{4,3,2,1,0:T(8,128)}, u32[]{:S(2)}) copy-start(f32[1,2,2,8,1024]{4,3,2,1,0:T(8,128)} %param.4) | copy-start | bytes 393220
where the time goes:
time: 158 us
  blocking collectives  87.5 us (55%)
  matrix products  23.6 us (15%)
  other arithmetic  20.7 us (13%)
  starting transfers between devices  19.4 us (12%)
  local copies, waits for them, and re-layouts  5.48 us (3%)
    psum x8, blocking collectives, psum_chan(): value = lax.psum(value, axis)  48.4 us
    psum x3, blocking collectives, psum_tm(): value = lax.psum(value, axis)  39.1 us
    dot_general x4, matrix products, disperse(): jnp.einsum('pcjq,cqn->pcjn', stacked, table, precision=lax.Precision.HIGH...  23.6 us
    ppermute x1, starting transfers between devices, on_device(): after = lax.ppermute(leading, TM, down)  12.6 us
    div x1, other arithmetic, tap_tables(): mat_im = sign * interior_part * symbol_profile * jnp.sin(turn) / scale  12.3 us
    ppermute x1, starting transfers between devices, on_device(): before = lax.ppermute(trailing, TM, up)  6.83 us
    concatenate x1, other arithmetic, merged_table(): return jnp.concatenate([top, bottom], axis=1)  5.14 us
  transfers between devices with their start and end apart: 2, of which 0 were waited for; matrix products, arithmetic and copies ran while one was open for 11% of the time, Pallas kernels for 0%

commit v1 on v0

--- a/solution.py
+++ b/solution.py
@@ -79,7 +79,7 @@
 
 def psum_chan(value):
     for axis in ("core", "ylo"):
-        value = lax.psum(value, axis)
+        value = jnp.sum(lax.all_gather(value, axis), axis=0)
     return value
 
 

time: 158 us -> 169 us (1.070)
  blocking collectives: 87.5 us -> 97.9 us
    all_gather x0 -> x8, blocking collectives: none -> 58.7 us  [psum_chan(): value = jnp.sum(lax.all_gather(value, axis), axis=0)]
    psum x8 -> x0, blocking collectives: 48.4 us -> none  [psum_chan(): value = lax.psum(value, axis)]
where the time goes in v1:
time: 169 us
  blocking collectives  97.9 us (58%)
  matrix products  23.6 us (14%)
  other arithmetic  20.9 us (12%)
  starting transfers between devices  19.4 us (11%)
  local copies, waits for them, and re-layouts  5.55 us (3%)
    all_gather x8, blocking collectives, psum_chan(): value = jnp.sum(lax.all_gather(value, axis), axis=0)  58.7 us
    psum x3, blocking collectives, psum_tm(): value = lax.psum(value, axis)  39.1 us
    dot_general x4, matrix products, disperse(): jnp.einsum('pcjq,cqn->pcjn', stacked, table, precision=lax.Precision.HIGH...  23.6 us
    ppermute x1, starting transfers between devices, on_device(): after = lax.ppermute(leading, TM, down)  12.6 us
    div x1, other arithmetic, tap_tables(): mat_im = sign * interior_part * symbol_profile * jnp.sin(turn) / scale  12.3 us
    ppermute x1, starting transfers between devices, on_device(): before = lax.ppermute(trailing, TM, up)  6.83 us
    concatenate x1, other arithmetic, merged_table(): return jnp.concatenate([top, bottom], axis=1)  5.14 us
  transfers between devices with their start and end apart: 2, of which 0 were waited for; matrix products, arithmetic and copies ran while one was open for 11% of the time, Pallas kernels for 0%

profile of v1, /device:TPU:8, one launch (start us, length us, event | category | flops | bytes accessed | tf_op | source)
XLA Modules:
  0.0 168.5 jit_solution(8352039086893406865)
XLA Ops:
  0.6 0.8 fusion.85
  1.4 0.9 fusion.84
  2.3 6.8 %collective-permute-start = (f32[2,2,8,768]{3,2,1,0:T(8,128)S(1)}, f32[2,2,8,768]{3,2,1,0:T(8,128)S(1)}, u32[]{:S(2)}, u32[]{:S(2)}) collective-permute-start(f32[2,2,8,768]{3,2,1,0:T(8,128)S(1)} %pad_maximum_fusion.2), channel_id=1, source_target_pairs={{0,8},{8,16},{16,24},{24,32},{32,40},{40,48},{48,56},{56,64},{64,7... | collective-permute-start | bytes 294920 | tf_op jit(solution)/shard_map/ppermute | solution.py:111
  9.2 12.6 %collective-permute-start.1 = (f32[2,2,8,768]{3,2,1,0:T(8,128)S(1)}, f32[2,2,8,768]{3,2,1,0:T(8,128)S(1)}, u32[]{:S(2)}, u32[]{:S(2)}) collective-permute-start(f32[2,2,8,768]{3,2,1,0:T(8,128)S(1)} %pad_maximum_fusion.3), channel_id=1, source_target_pairs={{8,0},{16,8},{24,16},{32,24},{40,32},{48,40},{56,48},{64,56},{72,6... | collective-permute-start | bytes 294920 | tf_op jit(solution)/shard_map/ppermute | solution.py:112
  22.0 0.2 exponential_reduce_fusion
  22.2 12.3 %fusion.27 = (f32[8,384,128]{2,1,0:T(8,128)S(1)}, f32[8,384,128]{2,1,0:T(8,128)S(1)}, f32[8,384,128]{2,1,0:T(8,128)S(1)}, f32[8,384,128]{2,1,0:T(8,128)S(1)}, f3...) fusion(f32[384,128]{1,0:T(8,128)S(1)} %fusion.62, f32[384,128]{1,0:T(8,128)S(1)} %broadcast_multiply_fusion.1, ...), kind=kLoop, calls=%fused_computation.33 | loop fusion | flops 9830400 | bytes 10223680 | tf_op jit(solution)/shard_map/div | solution.py:37
  34.5 5.1 %maximum_maximum_fusion = (f32[8,768,256]{2,1,0:T(8,128)}, f32[8,768,256]{2,1,0:T(8,128)}) fusion(f32[8,384,128]{2,1,0:T(8,128)S(1)} %get-tuple-element.39, f32[8,384,128]{2,1,0:T(8,128)S(1)} %get-tuple-element.40, f32[8,384,128]{2,1,0:T(8,128)S(1)} %get-tuple-element.41, f32[8,384,128]{2,1,0:T(8,128)S(1)} %get-tuple-element.38, ...), kind=kLoop, calls=%fused_computation | loop fusion | flops 9437184 | bytes 22020096 | tf_op jit(solution)/shard_map/concatenate | solution.py:44
  39.8 0.1 copy.89
  39.9 0.1 copy.90
  40.1 0.1 copy.91
  40.2 0.3 maximum_bitcast_fusion
  40.5 0.6 reshape.335
  41.0 6.1 %multiply_reduce_fusion.3 = (f32[14,256]{1,0:T(8,128)S(1)}, f32[8,14,256]{2,1,0:T(8,128)S(1)}, f32[2,8,14,256]{3,2,0,1:T(8,128)S(1)}) fusion(f32[2,8,14,768]{3,1,2,0:T(8,128)S(1)} %reshape.335, f32[8,768,256]{2,1,0:T(8,128)} %get-tuple-element.4), kind=kOutput, calls=%fused_computation.56 | convolution fusion | flops 528679424 | bytes 7337984 | tf_op jit(solution)/shard_map/pcjq,cqn->pcjn/dot_general | solution.py:56
  47.2 1.8 %all-gather.5 = f32[2,1,1792]{2,1,0:T(1,128)S(1)} all-gather(f32[1,1,1792]{2,1,0:T(1,128)S(1)} %reshape.348), channel_id=1, replica_groups=mesh['z'=4,'x'=8,'yh'=2,'ylo'=4,'core'=2] {'core'}, dimensions={0}, use_global_device_ids=true | all-gather | bytes 21504 | tf_op jit(solution)/shard_map/all_gather | solution.py:82
  49.1 11.7 %all-gather.6 = f32[4,1,1792]{2,1,0:T(1,128)S(1)} all-gather(f32[1,1,1792]{2,1,0:T(1,128)S(1)} %reshape.350), channel_id=2, replica_groups=mesh['z'=4,'x'=8,'yh'=2,'ylo'=4,'core'=2] {'ylo'}, dimensions={0}, use_global_device_ids=true | all-gather | bytes 35840 | tf_op jit(solution)/shard_map/all_gather | solution.py:82
  60.8 0.1 bitcast_reduce_fusion
  60.9 0.1 copy_bitcast_fusion
  61.1 0.2 fusion.66
  61.3 0.2 fusion.55
  61.6 0.4 fusion.53
  61.9 0.5 reshape.336
  62.4 6.1 %multiply_reduce_fusion.1 = (f32[12,256]{1,0:T(8,128)S(1)}, f32[8,12,256]{2,1,0:T(8,128)S(1)}, f32[2,8,12,256]{3,2,0,1:T(8,128)S(1)}) fusion(f32[2,8,12,768]{3,1,2,0:T(8,128)S(1)} %reshape.336, f32[8,768,256]{2,1,0:T(8,128)} %get-tuple-element.4), kind=kOutput, calls=%fused_computation.54 | convolution fusion | flops 453153792 | bytes 7188480 | tf_op jit(solution)/shard_map/pcjq,cqn->pcjn/dot_general | solution.py:56
  68.6 1.8 %all-gather.7 = f32[2,1,1536]{2,1,0:T(1,128)S(1)} all-gather(f32[1,1,1536]{2,1,0:T(1,128)S(1)} %reshape.352), channel_id=1, replica_groups=mesh['z'=4,'x'=8,'yh'=2,'ylo'=4,'core'=2] {'core'}, dimensions={0}, use_global_device_ids=true | all-gather | bytes 18432 | tf_op jit(solution)/shard_map/all_gather | solution.py:82
  70.4 13.2 %all-gather.8 = f32[4,1,1536]{2,1,0:T(1,128)S(1)} all-gather(f32[1,1,1536]{2,1,0:T(1,128)S(1)} %reshape.354), channel_id=3, replica_groups=mesh['z'=4,'x'=8,'yh'=2,'ylo'=4,'core'=2] {'ylo'}, dimensions={0}, use_global_device_ids=true | all-gather | bytes 30720 | tf_op jit(solution)/shard_map/all_gather | solution.py:82
  83.7 0.1 bitcast_reduce_fusion.1
  83.8 0.1 copy_bitcast_fusion.2
  83.9 0.2 fusion.71
  84.1 0.2 multiply_reduce_fusion.10
  84.3 8.8 %psum.21 = f32[3,8]{1,0:T(4,128)S(1)} all-reduce(f32[3,8]{1,0:T(4,128)S(1)} %pad_maximum_fusion.4), channel_id=1, replica_groups=mesh['z'=4,'x'=8,'yh'=2,'ylo'=4,'core'=2] {'yh'}, use_global_device_ids=true, to_apply=%region_16.0 | all-reduce | flops 24 | bytes 192 | tf_op jit(solution)/shard_map/psum | solution.py:76
  93.2 15.9 %psum.22 = f32[3,8]{1,0:T(4,128)S(1)} all-reduce(f32[3,8]{1,0:T(4,128)S(1)} %psum.21), channel_id=1, replica_groups=mesh['z'=4,'x'=8,'yh'=2,'ylo'=4,'core'=2] {'x'}, use_global_device_ids=true, to_apply=%region_17.0 | all-reduce | flops 24 | bytes 192 | tf_op jit(solution)/shard_map/psum | solution.py:76
  109.1 14.4 %psum.23 = f32[3,8]{1,0:T(4,128)S(1)} all-reduce(f32[3,8]{1,0:T(4,128)S(1)} %psum.22), channel_id=1, replica_groups=mesh['z'=4,'x'=8,'yh'=2,'ylo'=4,'core'=2] {'z'}, use_global_device_ids=true, to_apply=%region_18.0 | all-reduce | flops 24 | bytes 192 | tf_op jit(solution)/shard_map/psum | solution.py:76
  123.5 0.1 multiply_reduce_fusion.5
  123.7 1.8 %all-gather.9 = f32[2,1,1536]{2,1,0:T(1,128)S(1)} all-gather(f32[1,1,1536]{2,1,0:T(1,128)S(1)} %reshape.356), channel_id=4, replica_groups=mesh['z'=4,'x'=8,'yh'=2,'ylo'=4,'core'=2] {'core'}, dimensions={0}, use_global_device_ids=true | all-gather | bytes 18432 | tf_op jit(solution)/shard_map/all_gather | solution.py:82
  125.5 13.2 %all-gather.10 = f32[4,1,1536]{2,1,0:T(1,128)S(1)} all-gather(f32[1,1,1536]{2,1,0:T(1,128)S(1)} %reshape.358), channel_id=5, replica_groups=mesh['z'=4,'x'=8,'yh'=2,'ylo'=4,'core'=2] {'ylo'}, dimensions={0}, use_global_device_ids=true | all-gather | bytes 30720 | tf_op jit(solution)/shard_map/all_gather | solution.py:82
  138.8 0.2 fusion.69
  139.0 0.2 maximum_multiply_fusion
  139.2 0.1 fusion.82
  139.4 0.2 maximum_bitcast_fusion.1
  139.6 0.4 reshape.337
  140.0 6.0 %fusion.43 = f32[2,8,10,256]{3,2,0,1:T(8,128)S(1)} fusion(f32[8,768,256]{2,1,0:T(8,128)} %get-tuple-element.5, f32[2,8,10,768]{3,1,2,0:T(8,128)S(1)} %reshape.337), kind=kOutput, calls=%fused_computation.41 | convolution fusion | flops 377487360 | bytes 6946816 | tf_op jit(solution)/shard_map/pcjq,cqn->pcjn/dot_general | solution.py:56
  146.0 0.1 multiply_reduce_fusion.7
  146.1 1.8 %all-gather.11 = f32[2,1,1280]{2,1,0:T(1,128)S(1)} all-gather(f32[1,1,1280]{2,1,0:T(1,128)S(1)} %reshape.360), channel_id=1, replica_groups=mesh['z'=4,'x'=8,'yh'=2,'ylo'=4,'core'=2] {'core'}, dimensions={0}, use_global_device_ids=true | all-gather | bytes 15360 | tf_op jit(solution)/shard_map/all_gather | solution.py:82
  148.0 13.3 %all-gather.12 = f32[4,1,1280]{2,1,0:T(1,128)S(1)} all-gather(f32[1,1,1280]{2,1,0:T(1,128)S(1)} %reshape.362), channel_id=6, replica_groups=mesh['z'=4,'x'=8,'yh'=2,'ylo'=4,'core'=2] {'ylo'}, dimensions={0}, use_global_device_ids=true | all-gather | bytes 25600 | tf_op jit(solution)/shard_map/all_gather | solution.py:82
  161.3 0.2 fusion.74
  161.6 0.1 copy.85
  161.7 5.4 %fusion.46 = f32[2,2,8,8,128]{4,3,1,0,2:T(8,128)S(1)} fusion(f32[2,8,8,768]{3,2,0,1:T(8,128)S(1)} %bitcast.164, f32[8,768,256]{2,1,0:T(8,128)} %get-tuple-element.5), kind=kOutput, calls=%fused_computation.42 | convolution fusion | flops 301989888 | bytes 6815744 | tf_op jit(solution)/shard_map/pcjq,cqn->pcjn/dot_general | solution.py:56
  167.1 0.7 copy.115
  167.9 0.7 slice.152
  (57 shorter events, 0.9 us)
Async XLA Ops:
  0.6 21.4 %copy-start.2 = (s32[8]{0:T(128)S(1)}, s32[8]{0:T(128)}, u32[]{:S(2)}) copy-start(s32[8]{0:T(128)} %param.5) | copy-start | bytes 100
  2.3 37.3 %collective-permute-start = (f32[2,2,8,768]{3,2,1,0:T(8,128)S(1)}, f32[2,2,8,768]{3,2,1,0:T(8,128)S(1)}, u32[]{:S(2)}, u32[]{:S(2)}) collective-permute-start(f32[2,2,8,768]{3,2,1,0:T(8,128)S(1)} %pad_maximum_fusion.2), channel_id=1, source_target_pairs={{0,8},{8,16},{16,24},{24,32},{32,40},{40,48},{48,56},{56,64},{64,7... | collective-permute-start | bytes 294920 | tf_op jit(solution)/shard_map/ppermute | solution.py:111
  9.2 30.5 %collective-permute-start.1 = (f32[2,2,8,768]{3,2,1,0:T(8,128)S(1)}, f32[2,2,8,768]{3,2,1,0:T(8,128)S(1)}, u32[]{:S(2)}, u32[]{:S(2)}) collective-permute-start(f32[2,2,8,768]{3,2,1,0:T(8,128)S(1)} %pad_maximum_fusion.3), channel_id=1, source_target_pairs={{8,0},{16,8},{24,16},{32,24},{40,32},{48,40},{56,48},{64,56},{72,6... | collective-permute-start | bytes 294920 | tf_op jit(solution)/shard_map/ppermute | solution.py:112
  34.5 5.2 %copy-start.1 = (f32[2,2,8,1024]{3,2,1,0:T(8,128)S(1)}, f32[2,2,8,1024]{3,2,1,0:T(8,128)}, u32[]{:S(2)}) copy-start(f32[2,2,8,1024]{3,2,1,0:T(8,128)} %param.3) | copy-start | bytes 393220
  68.5 15.6 %copy-start = (f32[1,2,2,8,1024]{4,3,2,1,0:T(8,128)S(1)}, f32[1,2,2,8,1024]{4,3,2,1,0:T(8,128)}, u32[]{:S(2)}) copy-start(f32[1,2,2,8,1024]{4,3,2,1,0:T(8,128)} %param.4) | copy-start | bytes 393220
